TPU v7x, 256 devices: a whole 4x4x8 slice. The times are simulated.
256 devices in a mesh: section: 4 (over y), fsdp: 64 (over z, x, core).
Axes of the slice: x: 4, y: 4, z: 8, core: 2. Of those that a mesh axis runs over, the one named last changes fastest.
Arguments:
- acts: bfloat16 [4, 8192, 4096], P('section', 'fsdp'), may hold values from -6 to 6
- out_grad: bfloat16 [4, 8192, 1024], P('section', 'fsdp'), may hold values from -6 to 6
- norm_gain: float32 [4, 4096], P('section'), may hold values from 0.25 to 1.75
- tiles: bfloat16 [4, 512, 4096], P('section', 'fsdp'), may hold values from -0.25 to 0.25
- tile_cols: int32 [4, 64, 8], P('section'), may hold values from 0 to 15, as said below
- tile_count: int32 [4, 64], P('section'), may hold values from 3 to 8, as said below
- tile_store_slot: int32 [4, 512], P('section'), may hold values from 0 to 511, each once within a row
Outputs:
- handed: bfloat16 [4, 8192, 4096], P('section', 'fsdp')
- weight_grad: float32 [4, 512, 4096], P('section', 'fsdp')
Inputs may be any that keep to these rules, and one draw needn't show every extreme that they name: `tile_cols`: within a row panel the listed block columns are all different. `tile_count`: every section has a panel with exactly 8 and a panel with exactly 3 kept tiles. `tile_store_slot`: each section's row is a permutation of the slots.
All inputs are finite; a program needn't handle non-finite values.
Results may differ from a plain program's by a relative error of at most 0.0029.
Values may be sent and summed in bfloat16 or wider, within the bound.
No kernel may reach another device: no remote copies, remote signals or barrier semaphores. Data moves between devices by JAX's collectives and lax.ppermute only.
A program may use at most 128 MiB of HBM per device.

v0:
```python
import jax
import jax.numpy as jnp
from jax import lax
from jax.sharding import PartitionSpec as P

EPS = 1e-05


def shifted(value, axis, steps):
    count = lax.axis_size(axis)
    leading, last = (max(0, -steps), min(count, count - steps))
    return lax.ppermute(value, axis, [(source, source + steps) for source in range(leading, last)])


def local(acts, out_grad, norm_gain, tiles, tile_cols, tile_count, tile_store_slot):
    inputs_f = acts[0].astype(jnp.float32)
    key_grad = out_grad[0]
    gain_row = norm_gain[0]
    column_list = tile_cols[0]
    count_list = tile_count[0]
    slot_lookup = tile_store_slot[0]
    tok_rows, width = inputs_f.shape
    kv_width = key_grad.shape[1]
    panel_list, most_kept = column_list.shape
    blk = width // panel_list
    ncol = kv_width // blk
    store_slots = panel_list * most_kept
    area = blk * blk
    slot_dev = tiles.shape[1]
    grad_scale = (tok_rows * lax.axis_size("zx") * lax.axis_size("core")) ** (-0.5)
    tile_positions = jnp.arange(store_slots, dtype=jnp.int32)
    inverse_order = jnp.zeros((store_slots,), jnp.int32).at[slot_lookup].set(tile_positions)
    kept_grid = jnp.arange(most_kept)[None, :] < count_list[:, None]
    mean_sq = jnp.mean(inputs_f * inputs_f, axis=1, keepdims=True)
    recip = lax.rsqrt(mean_sq + EPS)
    normed = (inputs_f * recip * gain_row[None, :]).astype(jnp.bfloat16)
    zx_size = lax.axis_size("zx")
    core_size = lax.axis_size("core")
    gathered = lax.all_gather(tiles[0], "zx", axis=0, tiled=True)
    gathered = lax.all_gather(gathered, "core", axis=0, tiled=True)
    slot_ids = jnp.arange(store_slots, dtype=jnp.int32)
    slot_dev_i = slot_ids // (slot_dev * core_size)
    slot_core = slot_ids // slot_dev % core_size
    row_of_slot = slot_core * (zx_size * slot_dev) + slot_dev_i * slot_dev + slot_ids % slot_dev
    placed = gathered[row_of_slot[slot_lookup]].reshape(panel_list, most_kept, blk, blk)
    grad_padded = jnp.concatenate(
        [key_grad.reshape(tok_rows, ncol, blk), jnp.zeros((tok_rows, 1, blk), key_grad.dtype)],
        axis=1,
    )
    safe_cols = jnp.where(kept_grid, column_list, ncol)
    selected = grad_padded[:, safe_cols]
    normed_grad = jnp.einsum(
        "tpkb,pkab->tpa", selected, placed, preferred_element_type=jnp.float32
    ).reshape(tok_rows, width)
    normed_blocks = normed.reshape(tok_rows, panel_list, blk)
    terms_pos = jnp.einsum(
        "tpa,tpkb->pkab", normed_blocks, selected, preferred_element_type=jnp.float32
    )
    terms_pos = (terms_pos * grad_scale).reshape(store_slots, area)
    scaled = gain_row[None, :] * normed_grad
    inner = jnp.sum(scaled * inputs_f, axis=1, keepdims=True) / width
    input_grad = (recip * scaled - inputs_f * recip**3 * inner).astype(jnp.bfloat16)
    order_k = jnp.arange(core_size)[:, None, None]
    order_i = jnp.arange(zx_size)[None, :, None]
    order_j = jnp.arange(slot_dev)[None, None, :]
    rs_order = ((order_i * core_size + order_k) * slot_dev + order_j).reshape(-1)
    weight_grad = lax.psum_scatter(
        terms_pos[inverse_order[rs_order]], "core", scatter_dimension=0, tiled=True
    )
    weight_grad = lax.psum_scatter(weight_grad, "zx", scatter_dimension=0, tiled=True)
    handed = shifted(input_grad, "section", -1)
    return (handed[None], weight_grad[None])


def solution(mesh):
    sec, fs = mesh.devices.shape
    mesh = jax.sharding.Mesh(mesh.devices.reshape(sec, fs // 2, 2), ("section", "zx", "core"))
    F = ("zx", "core")
    placed = (
        P("section", F, None),
        P("section", F, None),
        P("section", None),
        P("section", F, None),
        P("section", None, None),
        P("section", None),
        P("section", None),
    )
    return jax.shard_map(
        local,
        mesh=mesh,
        in_specs=placed,
        out_specs=(P("section", F, None), P("section", F, None)),
        check_vma=False,
    )
```

profile of v0, /device:TPU:8, one launch (start us, length us, event | category | flops | bytes accessed | tf_op | source)
XLA Modules:
  0.0 460.3 jit_solution(11396080284697945354)
XLA Ops:
  7.2 0.0 copy-start.2
  7.2 0.0 copy-start.3
  7.2 0.0 all-gather.5.cloned.1.call-start
  7.2 0.7 all-gather.5.cloned.1.call-update
  7.9 0.0 all-gather.7.cloned.1.call-start
  8.0 83.4 %all-gather.5.cloned.1.call-done = bf16[1,256,4096]{2,1,0:T(8,128)(2,1)} async-done(((bf16[1,8,4096]{2,1,0:T(8,128)(2,1)}), bf16[1,256,4096]{2,1,0:T(8,128)(2,1)}) %all-gather.5.cloned.1.call-update) | async-done | bytes 2097168 | tf_op jit(solution)/shard_map/all_gather | solution.py:39
  91.4 0.0 all-gather.7.cloned.1.call-update
  91.4 0.0 reduce-scatter.3.cloned.1.call-start
  91.5 1.1 copy.12
  92.6 0.7 compare_select_fusion.4
  93.3 0.1 copy.13
  93.4 0.1 reshape.243
  93.5 1.5 copy.15
  95.0 0.5 broadcast.221
  95.5 0.0 copy-done.2
  95.5 0.7 reduce.4
  96.2 0.1 mul.116
  96.2 0.1 iota_add_fusion
  96.3 0.1 add.150
  96.4 0.0 copy-done.3
  96.5 3.5 gather_fusion
  100.0 0.0 copy-start.1
  100.0 13.4 %gather_fusion.2 = bf16[512,128,64]{1,2,0:T(8,128)(2,1)} fusion(bf16[128,17,64]{0,2,1:T(8,128)(2,1)S(1)} %concatenate.3, s32[1024]{0:T(1024)S(1)} %pad_clamp_fusion.2), kind=kCustom, calls=%fused_computation.2 | custom fusion | bytes 16779264 | tf_op jit(solution)/shard_map/gather | solution.py:51
  113.4 2.6 scatter_custom_fusion
  116.0 3.5 gather_fusion.3
  119.6 0.0 copy-done.1
  119.6 0.3 fusion.2
  119.9 0.0 all-gather.7.cloned.1.call-done
  119.9 11.3 %gather_fusion.1 = bf16[512,4096]{1,0:T(8,128)(2,1)} fusion(bf16[512,4096]{1,0:T(8,128)(2,1)} %bitcast.58, s32[1024]{0:T(1024)S(1)} %pad_clamp_fusion.3), kind=kCustom, calls=%fused_computation.1 | custom fusion | bytes 8390656 | tf_op jit(solution)/shard_map/gather | solution.py:45
  131.2 12.6 %reshape.220 = bf16[64,8,64,64]{3,2,1,0:T(8,128)(2,1)} reshape(bf16[512,4096]{1,0:T(8,128)(2,1)} %gather_fusion.1) | data formatting | bytes 8388608 | tf_op jit(solution)/shard_map/reshape | solution.py:45
  143.8 0.0 slice-start
  143.8 0.0 slice-start.1
  143.8 9.3 %fusion.1 = (f32[128]{0:T(128)S(1)}, f32[64,64,128,1]{2,1,3,0:T(8,128)}) fusion(f32[128,64,64]{0,2,1:T(8,128)S(1)} %bitcast.63, f32[64,64]{1,0:T(8,128)S(1)} %mul.116, bf16[64,8,64,64]{3,2,1,0:T(8,128)(2,1)} %reshape.220, bf16[128,64,8,64]{0,3,2,1:T(8,128)(2,1)} %bitcast.59), kind=kOutput, calls=%fused_computation.9 | convolution fusion | flops 538443648 | bytes 16794112 | tf_op jit(solution)/shard_map/tpkb,pkab->tpa/dot_general | solution.py:52
  153.1 0.0 slice-done
  153.1 0.0 slice-done.1
  153.1 7.1 %multiply_bitcast_fusion = f32[64,8,64,64]{2,3,1,0:T(8,128)} fusion(bf16[128,64,8,64]{0,3,2,1:T(8,128)(2,1)S(1)} %bitcast.62, f32[128,64,64]{0,2,1:T(8,128)S(1)} %bitcast.64, f32[128]{0:T(128)S(1)} %get-tuple-element.2, f32[64,64]{1,0:T(8,128)S(1)} %mul.116), kind=kOutput, calls=%fused_computation.6 | convolution fusion | flops 540540928 | bytes 18891264 | tf_op jit(solution)/shard_map/tpa,tpkb->pkab/dot_general | solution.py:56
  160.2 17.4 %copy.16 = f32[64,8,64,64]{3,2,1,0:T(8,128)} copy(f32[64,8,64,64]{2,3,1,0:T(8,128)} %multiply_bitcast_fusion) | data formatting | bytes 16777216 | tf_op jit(solution)/shard_map/mul | solution.py:59
  177.6 14.8 %reshape.222 = f32[512,4096]{1,0:T(8,128)} reshape(f32[64,8,64,64]{3,2,1,0:T(8,128)} %copy.16) | data formatting | bytes 16777216 | tf_op jit(solution)/shard_map/reshape | solution.py:59
  192.4 12.2 %gather_fusion.4 = f32[512,4096]{1,0:T(8,128)} fusion(f32[512,4096]{1,0:T(8,128)} %reshape.222, s32[1024]{0:T(1024)S(1)} %pad_clamp_fusion), kind=kCustom, calls=%fused_computation.4 | custom fusion | bytes 16779264 | tf_op jit(solution)/shard_map/gather | solution.py:68
  204.6 0.0 reduce-scatter.3.cloned.1.call-update
  204.7 0.0 copy-start
  204.7 0.0 reduce-scatter.5.cloned.1.call-start
  204.7 19.2 %reduce-scatter.3.cloned.1.call-done = f32[256,4096]{1,0:T(8,128)} async-done(((f32[512,4096]{1,0:T(8,128)}), f32[256,4096]{1,0:T(8,128)}) %reduce-scatter.3.cloned.1.call-update) | async-done | bytes 4194320 | tf_op jit(solution)/shard_map/reduce_scatter | solution.py:67
  223.9 0.0 reduce-scatter.5.cloned.1.call-update
  223.9 0.0 copy-done
  223.9 1.9 copy.14
  225.8 2.2 fusion.5
  228.0 2.7 collective-permute-start
  230.7 24.4 %collective-permute-done = bf16[128,4096]{1,0:T(8,128)(2,1)S(1)} collective-permute-done((bf16[128,4096]{1,0:T(8,128)(2,1)S(1)}, bf16[128,4096]{1,0:T(8,128)(2,1)S(1)}, u32[]{:S(2)}, u32[]{:S(2)}) %collective-permute-start) | collective-permute-done | bytes 1048608 | tf_op jit(solution)/shard_map/ppermute | solution.py:12
  255.1 197.6 %reduce-scatter.5.cloned.1.call-done = f32[8,4096]{1,0:T(8,128)} async-done(((f32[256,4096]{1,0:T(8,128)}), f32[8,4096]{1,0:T(8,128)}) %reduce-scatter.5.cloned.1.call-update) | async-done | bytes 131088 | tf_op jit(solution)/shard_map/reduce_scatter | solution.py:70
  452.8 1.0 copy.20
  (16 shorter events, 0.1 us)
Async XLA Ops:
  7.2 88.3 %copy-start.2 = (f32[1,4096]{1,0:T(1,128)S(1)}, f32[1,4096]{1,0:T(1,128)}, u32[]{:S(2)}) copy-start(f32[1,4096]{1,0:T(1,128)} %param.9) | copy-start | bytes 49156
  7.2 89.3 %copy-start.3 = (s32[1,512]{1,0:T(1,128)S(1)}, s32[1,512]{1,0:T(1,128)}, u32[]{:S(2)}) copy-start(s32[1,512]{1,0:T(1,128)} %param.13) | copy-start | bytes 6148
  7.2 84.2 %all-gather.5.cloned.1.call-start = ((), (), s32[]{:S(2)}) async-start(), calls=%async_computation.4 | async-start | bytes 2162688 | tf_op jit(solution)/shard_map/all_gather | solution.py:39
  7.9 112.0 %all-gather.7.cloned.1.call-start = ((), (), s32[]{:S(2)}) async-start(), calls=%async_computation.5 | async-start | bytes 6291456 | tf_op jit(solution)/shard_map/all_gather | solution.py:40
  91.4 132.5 %reduce-scatter.3.cloned.1.call-start = ((), (), s32[]{:S(2)}) async-start(), calls=%async_computation.2 | async-start | bytes 12582912 | tf_op jit(solution)/shard_map/reduce_scatter | solution.py:67
  100.0 19.6 %copy-start.1 = (bf16[1,128,4096]{2,1,0:T(8,128)(2,1)S(1)}, bf16[1,128,4096]{2,1,0:T(8,128)(2,1)}, u32[]{:S(2)}) copy-start(bf16[1,128,4096]{2,1,0:T(8,128)(2,1)} %param.7) | copy-start | bytes 3145732
  143.8 9.3 %slice-start = ((s8[8388608]{0:T(1024)(128)(4,1)}), s8[4194304]{0:T(1024)(128)(4,1)S(1)}, s32[]{:S(2)}) async-start(s8[8388608]{0:T(1024)(128)(4,1)} %bitcast.60), calls=%async_computation.6 | async-start | bytes 8388608
  143.8 9.3 %slice-start.1 = ((s8[8388608]{0:T(1024)(128)(4,1)}), s8[4194304]{0:T(1024)(128)(4,1)S(1)}, s32[]{:S(2)}) async-start(s8[8388608]{0:T(1024)(128)(4,1)} %bitcast.60), calls=%async_computation.7 | async-start | bytes 8388608
  204.7 19.2 %copy-start = (f32[64,64,128,1]{2,1,3,0:T(8,128)S(1)}, f32[64,64,128,1]{2,1,3,0:T(8,128)}, u32[]{:S(2)}) copy-start(f32[64,64,128,1]{2,1,3,0:T(8,128)} %get-tuple-element.5) | copy-start | bytes 6291460
  204.7 248.1 %reduce-scatter.5.cloned.1.call-start = ((), (), s32[]{:S(2)}) async-start(), calls=%async_computation.3 | async-start | bytes 4325376 | tf_op jit(solution)/shard_map/reduce_scatter | solution.py:70
  228.0 27.1 %collective-permute-start = (bf16[128,4096]{1,0:T(8,128)(2,1)S(1)}, bf16[128,4096]{1,0:T(8,128)(2,1)S(1)}, u32[]{:S(2)}, u32[]{:S(2)}) collective-permute-start(bf16[128,4096]{1,0:T(8,128)(2,1)S(1)} %fusion.5), channel_id=1, source_target_pairs={{64,0},{128,64},{192,128},{65,1},{129,65},{193,129},{66,2},{130,66... | collective-permute-start | bytes 3145736 | tf_op jit(solution)/shard_map/ppermute | solution.py:12
Sparse Core Ops, SparseCore 0:
  10.6 80.7 all-gather.4
  93.2 16.2 all-gather.6
  204.8 19.0 reduce-scatter.2
  228.2 224.5 reduce-scatter.4
where the time goes:
time: 461 us; the launch traced here: 460 us
  waiting for transfers between devices  325 us (70%)
  local copies, waits for them, and re-layouts  97.6 us (21%)
  matrix products  16.4 us (4%)
  between operations  14 us (3%)
    reduce_scatter x1, waiting for transfers between devices, local(): lax.psum_scatter(weight_grad, 'zx', scatter_dimension=0, tiled=True)  198 us
    all_gather x1, waiting for transfers between devices, local(): gathered = lax.all_gather(tiles[0], 'zx', axis=0, tiled=True)  83.4 us
    ppermute x1, waiting for transfers between devices, shifted(): lax.ppermute(value, axis, [(source, source + steps) for source in range(l...  24.4 us
    reduce_scatter x1, waiting for transfers between devices, local(): lax.psum_scatter(terms_pos[inverse_order[rs_order]], 'core', scatter_dime...  19.2 us
    mul x1, local copies, waits for them, and re-layouts, local(): terms_pos = (terms_pos * grad_scale).reshape(store_slots, area)  17.4 us
    reshape x1, local copies, waits for them, and re-layouts, local(): terms_pos = (terms_pos * grad_scale).reshape(store_slots, area)  14.8 us
    gather x1, local copies, waits for them, and re-layouts, local(): selected = grad_padded[:, safe_cols]  13.4 us
    reshape x1, local copies, waits for them, and re-layouts, local(): gathered[row_of_slot[slot_lookup]].reshape(panel_list, most_kept, blk, blk)  12.6 us
  transfers between devices with their start and end apart: 5, of which 4 were waited for; matrix products, arithmetic and copies ran while one was open for 7% of the time, Pallas kernels for 0%

commit v1 on v0

--- a/solution.py
+++ b/solution.py
@@ -36,7 +36,9 @@
     normed = (inputs_f * recip * gain_row[None, :]).astype(jnp.bfloat16)
     zx_size = lax.axis_size("zx")
     core_size = lax.axis_size("core")
-    gathered = lax.all_gather(tiles[0], "zx", axis=0, tiled=True)
+    gathered = jnp.concatenate(
+        lax.all_to_all(jnp.stack(lax.axis_size("zx") * [tiles[0]], axis=0), "zx", 0, 0), axis=0
+    )
     gathered = lax.all_gather(gathered, "core", axis=0, tiled=True)
     slot_ids = jnp.arange(store_slots, dtype=jnp.int32)
     slot_dev_i = slot_ids // (slot_dev * core_size)

time: 461 us -> 439 us (0.952)
  waiting for transfers between devices: 325 us -> 242 us
  blocking collectives: 0 us -> 61.7 us
    all_gather x1 -> x0, waiting for transfers between devices: 83.4 us -> none  [local(): gathered = lax.all_gather(tiles[0], 'zx', axis=0, tiled=True)]
    all_to_all x0 -> x1, blocking collectives: none -> 61.7 us  [local(): lax.all_to_all(jnp.stack(lax.axis_size('zx') * [tiles[0]], axis=0), 'zx',...]
  transfers between devices with their start and end apart: 5 -> 4, of which waited for: 4 -> 3; matrix products, arithmetic and copies ran while one was open for 7% -> 7% of each run, Pallas kernels for 0% -> 0%
where the time goes in v1:
time: 439 us; the launch traced here: 438 us
  waiting for transfers between devices  242 us (55%)
  local copies, waits for them, and re-layouts  98.5 us (22%)
  blocking collectives  61.7 us (14%)
  matrix products  16.4 us (4%)
  between operations  14 us (3%)
    reduce_scatter x1, waiting for transfers between devices, local(): lax.psum_scatter(weight_grad, 'zx', scatter_dimension=0, tiled=True)  198 us
    all_to_all x1, blocking collectives, local(): lax.all_to_all(jnp.stack(lax.axis_size('zx') * [tiles[0]], axis=0), 'zx',...  61.7 us
    ppermute x1, waiting for transfers between devices, shifted(): lax.ppermute(value, axis, [(source, source + steps) for source in range(l...  24.4 us
    reduce_scatter x1, waiting for transfers between devices, local(): lax.psum_scatter(terms_pos[inverse_order[rs_order]], 'core', scatter_dime...  19.1 us
    mul x1, local copies, waits for them, and re-layouts, local(): terms_pos = (terms_pos * grad_scale).reshape(store_slots, area)  17.4 us
    reshape x1, local copies, waits for them, and re-layouts, local(): terms_pos = (terms_pos * grad_scale).reshape(store_slots, area)  14.8 us
    gather x1, local copies, waits for them, and re-layouts, local(): selected = grad_padded[:, safe_cols]  13.4 us
    reshape x1, local copies, waits for them, and re-layouts, local(): gathered[row_of_slot[slot_lookup]].reshape(panel_list, most_kept, blk, blk)  12.6 us
  transfers between devices with their start and end apart: 4, of which 3 were waited for; matrix products, arithmetic and copies ran while one was open for 7% of the time, Pallas kernels for 0%

profile of v1, /device:TPU:8, one launch (start us, length us, event | category | flops | bytes accessed | tf_op | source)
XLA Modules:
  0.0 438.4 jit_solution(12646975113457193823)
XLA Ops:
  7.2 0.0 all-gather.2.cloned.1.call-start
  7.2 0.0 copy-start.2
  7.2 0.0 copy-start.4
  7.2 0.0 copy-start.6
  7.2 0.0 copy-start.1
  7.3 1.2 stack.3
  8.4 0.0 copy-start.3
  8.4 0.0 copy-start.5
  8.4 61.7 %all_to_all.5 = bf16[32,8,4096]{2,1,0:T(8,128)(2,1)} all-to-all(bf16[32,8,4096]{2,1,0:T(8,128)(2,1)S(1)} %stack.3), channel_id=1, replica_groups=mesh['section'=4,'zx'=32,'core'=2] {'zx'}, dimensions={0} | all-to-all | bytes 4194304 | tf_op jit(solution)/shard_map/all_to_all | solution.py:40
  70.2 0.0 all-gather.2.cloned.1.call-update
  70.2 0.0 reduce-scatter.3.cloned.1.call-start
  70.3 0.0 copy-done.2
  70.3 0.8 copy.12
  71.1 0.0 copy-done.4
  71.1 0.0 copy-done.6
  71.1 0.1 copy.13
  71.2 0.1 reshape.248
  71.3 0.0 copy-done.1
  71.3 0.5 copy.15
  71.8 0.5 broadcast.222
  72.4 0.0 copy-done.3
  72.4 0.7 reduce.4
  73.1 0.1 mul.116
  73.1 0.1 iota_add_fusion
  73.2 0.1 add.150
  73.3 0.0 copy-done.5
  73.4 3.5 gather_fusion
  76.9 1.0 concatenate.3
  77.9 13.4 %gather_fusion.2 = bf16[512,128,64]{1,2,0:T(8,128)(2,1)} fusion(bf16[128,17,64]{0,2,1:T(8,128)(2,1)S(1)} %concatenate.3, s32[1024]{0:T(1024)S(1)} %pad_clamp_fusion.2), kind=kCustom, calls=%fused_computation.2 | custom fusion | bytes 16779264 | tf_op jit(solution)/shard_map/gather | solution.py:53
  91.2 2.6 scatter_custom_fusion
  93.9 3.5 gather_fusion.3
  97.4 0.3 fusion.2
  97.7 0.0 all-gather.2.cloned.1.call-done
  97.7 11.3 %gather_fusion.1 = bf16[512,4096]{1,0:T(8,128)(2,1)} fusion(bf16[512,4096]{1,0:T(8,128)(2,1)} %all-gather.2.cloned.1.call-done, s32[1024]{0:T(1024)S(1)} %pad_clamp_fusion.3), kind=kCustom, calls=%fused_computation.1 | custom fusion | bytes 8390656 | tf_op jit(solution)/shard_map/gather | solution.py:47
  109.0 12.6 %reshape.225 = bf16[64,8,64,64]{3,2,1,0:T(8,128)(2,1)} reshape(bf16[512,4096]{1,0:T(8,128)(2,1)} %gather_fusion.1) | data formatting | bytes 8388608 | tf_op jit(solution)/shard_map/reshape | solution.py:47
  121.6 0.0 slice-start
  121.6 0.0 slice-start.1
  121.6 9.3 %fusion.1 = (f32[128]{0:T(128)S(1)}, f32[64,64,128,1]{2,1,3,0:T(8,128)}) fusion(f32[128,64,64]{0,2,1:T(8,128)S(1)} %bitcast.63, f32[64,64]{1,0:T(8,128)S(1)} %mul.116, bf16[64,8,64,64]{3,2,1,0:T(8,128)(2,1)} %reshape.225, bf16[128,64,8,64]{0,3,2,1:T(8,128)(2,1)} %bitcast.59), kind=kOutput, calls=%fused_computation.9 | convolution fusion | flops 538443648 | bytes 16794112 | tf_op jit(solution)/shard_map/tpkb,pkab->tpa/dot_general | solution.py:54
  130.9 0.0 slice-done
  130.9 0.0 slice-done.1
  131.0 7.1 %multiply_bitcast_fusion = f32[64,8,64,64]{2,3,1,0:T(8,128)} fusion(bf16[128,64,8,64]{0,3,2,1:T(8,128)(2,1)S(1)} %bitcast.62, f32[128,64,64]{0,2,1:T(8,128)S(1)} %bitcast.64, f32[128]{0:T(128)S(1)} %get-tuple-element.2, f32[64,64]{1,0:T(8,128)S(1)} %mul.116), kind=kOutput, calls=%fused_computation.6 | convolution fusion | flops 540540928 | bytes 18891264 | tf_op jit(solution)/shard_map/tpa,tpkb->pkab/dot_general | solution.py:58
  138.0 17.4 %copy.16 = f32[64,8,64,64]{3,2,1,0:T(8,128)} copy(f32[64,8,64,64]{2,3,1,0:T(8,128)} %multiply_bitcast_fusion) | data formatting | bytes 16777216 | tf_op jit(solution)/shard_map/mul | solution.py:61
  155.5 14.8 %reshape.227 = f32[512,4096]{1,0:T(8,128)} reshape(f32[64,8,64,64]{3,2,1,0:T(8,128)} %copy.16) | data formatting | bytes 16777216 | tf_op jit(solution)/shard_map/reshape | solution.py:61
  170.2 12.2 %gather_fusion.4 = f32[512,4096]{1,0:T(8,128)} fusion(f32[512,4096]{1,0:T(8,128)} %reshape.227, s32[1024]{0:T(1024)S(1)} %pad_clamp_fusion), kind=kCustom, calls=%fused_computation.4 | custom fusion | bytes 16779264 | tf_op jit(solution)/shard_map/gather | solution.py:70
  182.5 0.0 reduce-scatter.3.cloned.1.call-update
  182.5 0.0 copy-start
  182.5 0.0 reduce-scatter.5.cloned.1.call-start
  182.5 19.1 %reduce-scatter.3.cloned.1.call-done = f32[256,4096]{1,0:T(8,128)} async-done(((f32[512,4096]{1,0:T(8,128)}), f32[256,4096]{1,0:T(8,128)}) %reduce-scatter.3.cloned.1.call-update) | async-done | bytes 4194320 | tf_op jit(solution)/shard_map/reduce_scatter | solution.py:69
  201.6 0.0 reduce-scatter.5.cloned.1.call-update
  201.6 0.0 copy-done
  201.6 1.9 copy.14
  203.5 2.2 fusion.5
  205.7 2.7 collective-permute-start
  208.4 24.4 %collective-permute-done = bf16[128,4096]{1,0:T(8,128)(2,1)S(1)} collective-permute-done((bf16[128,4096]{1,0:T(8,128)(2,1)S(1)}, bf16[128,4096]{1,0:T(8,128)(2,1)S(1)}, u32[]{:S(2)}, u32[]{:S(2)}) %collective-permute-start) | collective-permute-done | bytes 1048608 | tf_op jit(solution)/shard_map/ppermute | solution.py:12
  232.9 198.0 %reduce-scatter.5.cloned.1.call-done = f32[8,4096]{1,0:T(8,128)} async-done(((f32[256,4096]{1,0:T(8,128)}), f32[8,4096]{1,0:T(8,128)}) %reduce-scatter.5.cloned.1.call-update) | async-done | bytes 131088 | tf_op jit(solution)/shard_map/reduce_scatter | solution.py:72
  430.9 1.0 copy.20
  (16 shorter events, 0.1 us)
Async XLA Ops:
  7.2 90.6 %all-gather.2.cloned.1.call-start = ((), (), s32[]{:S(2)}) async-start(), calls=%async_computation.3 | async-start | bytes 6291456 | tf_op jit(solution)/shard_map/all_gather | solution.py:42
  7.2 63.1 %copy-start.2 = (bf16[1,128,1024]{2,1,0:T(8,128)(2,1)S(1)}, bf16[1,128,1024]{2,1,0:T(8,128)(2,1)}, u32[]{:S(2)}) copy-start(bf16[1,128,1024]{2,1,0:T(8,128)(2,1)} %param.8) | copy-start | bytes 786436
  7.2 63.9 %copy-start.4 = (s32[1,64,8]{1,2,0:T(8,128)S(1)}, s32[1,64,8]{1,2,0:T(8,128)}, u32[]{:S(2)}) copy-start(s32[1,64,8]{1,2,0:T(8,128)} %param.11) | copy-start | bytes 6148
  7.2 63.9 %copy-start.6 = (s32[1,64]{1,0:T(1,128)S(1)}, s32[1,64]{1,0:T(1,128)}, u32[]{:S(2)}) copy-start(s32[1,64]{1,0:T(1,128)} %param.12) | copy-start | bytes 772
  7.2 64.1 %copy-start.1 = (bf16[1,128,4096]{2,1,0:T(8,128)(2,1)S(1)}, bf16[1,128,4096]{2,1,0:T(8,128)(2,1)}, u32[]{:S(2)}) copy-start(bf16[1,128,4096]{2,1,0:T(8,128)(2,1)} %param.7) | copy-start | bytes 3145732
  8.4 63.9 %copy-start.3 = (f32[1,4096]{1,0:T(1,128)S(1)}, f32[1,4096]{1,0:T(1,128)}, u32[]{:S(2)}) copy-start(f32[1,4096]{1,0:T(1,128)} %param.9) | copy-start | bytes 49156
  8.4 64.9 %copy-start.5 = (s32[1,512]{1,0:T(1,128)S(1)}, s32[1,512]{1,0:T(1,128)}, u32[]{:S(2)}) copy-start(s32[1,512]{1,0:T(1,128)} %param.13) | copy-start | bytes 6148
  70.2 131.4 %reduce-scatter.3.cloned.1.call-start = ((), (), s32[]{:S(2)}) async-start(), calls=%async_computation.4 | async-start | bytes 12582912 | tf_op jit(solution)/shard_map/reduce_scatter | solution.py:69
  121.6 9.3 %slice-start = ((s8[8388608]{0:T(1024)(128)(4,1)}), s8[4194304]{0:T(1024)(128)(4,1)S(1)}, s32[]{:S(2)}) async-start(s8[8388608]{0:T(1024)(128)(4,1)} %bitcast.60), calls=%async_computation.6 | async-start | bytes 8388608
  121.6 9.3 %slice-start.1 = ((s8[8388608]{0:T(1024)(128)(4,1)}), s8[4194304]{0:T(1024)(128)(4,1)S(1)}, s32[]{:S(2)}) async-start(s8[8388608]{0:T(1024)(128)(4,1)} %bitcast.60), calls=%async_computation.7 | async-start | bytes 8388608
  182.5 19.2 %copy-start = (f32[64,64,128,1]{2,1,3,0:T(8,128)S(1)}, f32[64,64,128,1]{2,1,3,0:T(8,128)}, u32[]{:S(2)}) copy-start(f32[64,64,128,1]{2,1,3,0:T(8,128)} %get-tuple-element.5) | copy-start | bytes 6291460
  182.5 248.4 %reduce-scatter.5.cloned.1.call-start = ((), (), s32[]{:S(2)}) async-start(), calls=%async_computation.5 | async-start | bytes 4325376 | tf_op jit(solution)/shard_map/reduce_scatter | solution.py:72
  205.7 27.1 %collective-permute-start = (bf16[128,4096]{1,0:T(8,128)(2,1)S(1)}, bf16[128,4096]{1,0:T(8,128)(2,1)S(1)}, u32[]{:S(2)}, u32[]{:S(2)}) collective-permute-start(bf16[128,4096]{1,0:T(8,128)(2,1)S(1)} %fusion.5), channel_id=1, source_target_pairs={{64,0},{128,64},{192,128},{65,1},{129,65},{193,129},{66,2},{130,66... | collective-permute-start | bytes 3145736 | tf_op jit(solution)/shard_map/ppermute | solution.py:12
Sparse Core Ops, SparseCore 0:
  70.3 16.1 all-gather.1
  182.6 18.9 reduce-scatter.2
  206.1 224.7 reduce-scatter.4
